TPU v7x, 128 devices: a whole 4x4x4 slice. The times are simulated.
128 devices in a mesh: ctx: 16 (over x, y_hi, core), head: 8 (over z, y_lo).
Axes of the slice: x: 4, y: 4 (y_hi: 2, y_lo: 2; y = y_hi * 2 + y_lo), z: 4, core: 2. Of those that a mesh axis runs over, the one named last changes fastest.
Arguments:
- activations: bfloat16 [8192, 4096], P('ctx')
- qkv_weight: bfloat16 [4096, 3, 32, 128], P(None, None, 'head'), may hold values from -0.09375 to 0.09375
- out_weight: bfloat16 [32, 128, 4096], P('head'), may hold values from -0.09375 to 0.09375
- mod_table: float32 [16, 4096], replicated, may hold values from -3 to 3
- clip_level: int32 [64], replicated, may hold values from 0 to 15
- clip_of: int32 [8192], P('ctx'), may hold values from 0 to 63, never falling along the last dimension, each value on 1 to 256 neighbouring positions
- visible: int32 [64, 64], replicated, may hold values from 0 to 1, as said below
Outputs:
- mixed: bfloat16 [8192, 4096], P(('ctx', 'head'))
Inputs may be any that keep to these rules, and one draw needn't show every extreme that they name: visible is 1 on the diagonal and 0 above it. `clip_of`: clip numbers never fall along the tokens; every clip has 1 to 256 tokens and one has exactly 256.
All inputs are finite; a program needn't handle non-finite values.
Results may differ from a plain program's by a relative error of at most 0.02.
The roundings to bfloat16 on the way count: a program that leaves them out, or rounds other values in their place, can miss the bound.
Values may be sent and summed in bfloat16 or wider, within the bound.
No kernel may reach another device: no remote copies, remote signals or barrier semaphores. Data moves between devices by JAX's collectives and lax.ppermute only.
A program may use at most 128 MiB of HBM per device.

v0:
```python
import math
import jax
import jax.numpy as jnp
from jax import lax
from jax.sharding import PartitionSpec as P


def score_block(state_now, kv_block, key_clips, queries, query_vis, score_scale):
    clip_count = query_vis.shape[1]
    clip_ids = lax.broadcasted_iota(jnp.int32, (1, clip_count), 1)
    key_hot = (key_clips[:, None] == clip_ids).astype(jnp.float32)
    allowed = jnp.dot(query_vis, key_hot.T, precision=lax.Precision.HIGHEST) > 0.5
    top_score, totals, summed = state_now
    key_rows = kv_block[:, 0]
    value_rows = kv_block[:, 1]
    scores = (
        jnp.einsum("rhd,khd->hrk", queries, key_rows, preferred_element_type=jnp.float32)
        * score_scale
    )
    masked = jnp.where(allowed[None], scores, -1e30)
    new_top = jnp.maximum(top_score, jnp.max(masked, axis=2))
    weights = jnp.where(allowed[None], jnp.exp(masked - new_top[:, :, None]), 0.0)
    factor = jnp.exp(top_score - new_top)
    totals = totals * factor + jnp.sum(weights, axis=2)
    summed = summed * factor[:, :, None] + jnp.einsum(
        "hrk,khd->hrd", weights.astype(jnp.bfloat16), value_rows, preferred_element_type=jnp.float32
    )
    return (new_top, totals, summed)


def fold_keys(state_now, kv_rows, key_clips, queries, query_vis, score_scale):
    key_count = kv_rows.shape[0]
    block_rows = math.gcd(key_count, 512)

    def one_block(block_index, state_in):
        first_row = block_index * block_rows
        kv_block = lax.dynamic_slice_in_dim(kv_rows, first_row, block_rows, 0)
        clip_block = lax.dynamic_slice_in_dim(key_clips, first_row, block_rows, 0)
        return score_block(state_in, kv_block, clip_block, queries, query_vis, score_scale)

    return lax.fori_loop(0, key_count // block_rows, one_block, state_now)


def per_device(activations, qkv_weight, out_weight, mod_table, clip_level, clip_of, visible):
    heads_here = qkv_weight.shape[2]
    head_size = qkv_weight.shape[3]
    clip_count = visible.shape[0]
    level_count = mod_table.shape[0]
    clip_ids = lax.broadcasted_iota(jnp.int32, (1, clip_count), 1)
    level_ids = lax.broadcasted_iota(jnp.int32, (1, level_count), 1)
    tok_hot = clip_of[:, None] == clip_ids
    level_rows = jnp.sum(jnp.where(tok_hot, clip_level[None, :], 0), axis=1)
    level_hot = (level_rows[:, None] == level_ids).astype(jnp.float32)
    modulation = jnp.dot(level_hot, mod_table, precision=lax.Precision.HIGHEST)
    moduled = (activations.astype(jnp.float32) * (1.0 + modulation)).astype(jnp.bfloat16)
    qkv = jnp.einsum(
        "td,dchk->tchk", moduled, qkv_weight, preferred_element_type=jnp.float32
    ).astype(jnp.bfloat16)
    queries = qkv[:, 0]
    kv_local = qkv[:, 1:3]
    query_count = queries.shape[0]
    query_hot = (clip_of[:, None] == clip_ids).astype(jnp.float32)
    query_vis = jnp.dot(query_hot, visible.astype(jnp.float32), precision=lax.Precision.HIGHEST)
    score_scale = 1.0 / jnp.sqrt(jnp.float32(head_size))
    initial = (
        jnp.full((heads_here, query_count), -1e30, jnp.float32),
        jnp.zeros((heads_here, query_count), jnp.float32),
        jnp.zeros((heads_here, query_count, head_size), jnp.float32),
    )
    kv_all, clips_all = (
        lax.all_gather(kv_local, "ctx", axis=0, tiled=True),
        lax.all_gather(clip_of, "ctx", axis=0, tiled=True),
    )
    final = fold_keys(initial, kv_all, clips_all, queries, query_vis, score_scale)
    attended = (final[2] / final[1][:, :, None]).astype(jnp.bfloat16)
    attended_rows = jnp.transpose(attended, (1, 0, 2))
    return lax.psum_scatter(
        jnp.einsum(
            "rhd,hdo->ro", attended_rows, out_weight, preferred_element_type=jnp.float32
        ).astype(jnp.bfloat16),
        "head",
        scatter_dimension=0,
        tiled=True,
    )


def solution(mesh):
    placed = (
        P("ctx", None),
        P(None, None, "head", None),
        P("head", None, None),
        P(),
        P(),
        P("ctx"),
        P(),
    )
    return jax.shard_map(
        per_device, mesh=mesh, in_specs=placed, out_specs=P(("ctx", "head"), None), check_vma=False
    )
```

profile of v0, /device:TPU:1, one launch (start us, length us, event | category | flops | bytes accessed | tf_op | source)
XLA Modules:
  0.0 363.7 jit_solution(15202667989823776024)
XLA Ops:
  7.5 5.6 %fusion.20 = bf16[512,4096,1,1]{1,0,3,2:T(8,128)(2,1)S(1)} fusion(f32[16,4096]{1,0:T(8,128)S(1)} %copy-done, bf16[512,4096]{1,0:T(8,128)(2,1)} %param.9, s32[512]{0:T(512)S(1)} %select_reduce_fusion), kind=kOutput, calls=%fused_computation.29 | convolution fusion | flops 411049984 | bytes 8652800 | tf_op jit(solution)/shard_map/dot_general | solution.py:54
  13.1 10.1 %fusion.21 = bf16[512,3,4,128]{3,0,2,1:T(8,128)(2,1)S(1)} fusion(bf16[512,4096,1,1]{1,0,3,2:T(8,128)(2,1)S(1)} %fusion.20, bf16[4096,3,4,128]{3,2,1,0:T(4,128)(2,1)} %param.10), kind=kOutput, calls=%fused_computation.30 | convolution fusion | flops 6443237376 | bytes 18350080 | tf_op jit(solution)/shard_map/td,dchk->tchk/dot_general | solution.py:56
  24.4 26.2 %all-gather = s32[16,1,512]{2,1,0:T(1,128)S(1)} all-gather(s32[1,1,512]{2,1,0:T(1,128)S(1)} %bitcast.58), channel_id=1, replica_groups=mesh['ctx'=16,'head'=8] {'ctx'}, dimensions={0}, use_global_device_ids=true | all-gather | bytes 34816 | tf_op jit(solution)/shard_map/all_gather | solution.py:72
  51.1 86.8 %all-gather.3.cloned.1.call-done = bf16[8192,2,4,128]{3,0,2,1:T(8,128)(2,1)} async-done(((bf16[512,2,4,128]{3,0,2,1:T(8,128)(2,1)}), bf16[8192,2,4,128]{3,0,2,1:T(8,128)(2,1)}) %all-gather.3.cloned.1.call-update) | async-done | bytes 16777232 | tf_op jit(solution)/shard_map/all_gather | solution.py:71
  137.9 123.4 %while.18 = (s32[]{:T(128)}, f32[4,512]{1,0:T(4,128)S(1)}, f32[4,512]{1,0:T(4,128)S(1)}, f32[4,512,128]{2,1,0:T(8,128)}, s32[8192]{0:T(1024)S(1)}, /*index=5*/f3...) while((s32[]{:T(128)}, f32[4,512]{1,0:T(4,128)S(1)}, ...), condition=%wide.region_4.5_spmd.clone, body=%wide.region_1.4_spmd.clone.sunk | while | flops 752920576 | bytes 25958676 | solution.py:41
  138.7 2.0 fusion.46
  141.8 2.9 fusion.49
  146.4 2.0 fusion.46
  149.5 2.9 fusion.49
  154.1 2.0 fusion.46
  157.2 2.9 fusion.49
  161.8 2.0 fusion.46
  164.9 2.9 fusion.49
  169.5 2.0 fusion.46
  172.6 2.9 fusion.49
  177.2 2.0 fusion.46
  180.3 2.9 fusion.49
  184.9 2.0 fusion.46
  188.1 2.9 fusion.49
  192.7 2.0 fusion.46
  195.8 2.9 fusion.49
  200.4 2.0 fusion.46
  203.5 2.9 fusion.49
  211.2 2.9 fusion.49
  218.9 2.9 fusion.49
  226.6 2.9 fusion.49
  234.3 2.9 fusion.49
  242.1 2.9 fusion.49
  249.8 2.9 fusion.49
  257.5 2.9 fusion.49
  261.3 6.9 %bitcast_convert_fusion = bf16[512,4096]{1,0:T(8,128)(2,1)} fusion(bf16[4,128,4096]{2,1,0:T(8,128)(2,1)} %param.11, f32[4,512,128]{2,1,0:T(8,128)} %get-tuple-element.145, f32[4,512]{1,0:T(4,128)S(1)} %get-tuple-element.146), kind=kOutput, calls=%fused_computation.27 | convolution fusion | flops 2150105088 | bytes 9445376 | tf_op jit(solution)/shard_map/rhd,hdo->ro/dot_general | solution.py:78
  268.2 88.6 %reduce-scatter.2.cloned.1.call-done = bf16[64,4096]{1,0:T(8,128)(2,1)} async-done(((bf16[512,4096]{1,0:T(8,128)(2,1)}), bf16[64,4096]{1,0:T(8,128)(2,1)}) %reduce-scatter.2.cloned.1.call-update) | async-done | bytes 524304 | tf_op jit(solution)/shard_map/reduce_scatter | solution.py:77
  (184 shorter events, 61.0 us)
Async XLA Ops:
  6.5 1.0 copy-start
  6.5 131.4 %all-gather.3.cloned.1.call-start = ((), (), s32[]{:S(2)}) async-start(), calls=%async_computation.1 | async-start | bytes 17825792 | tf_op jit(solution)/shard_map/all_gather | solution.py:71
  13.1 11.3 %copy-start.2 = (s32[512]{0:T(512)S(1)}, s32[512]{0:T(512)}, u32[]{:S(2)}) copy-start(s32[512]{0:T(512)} %param.14) | copy-start | bytes 6148
  13.1 37.5 %copy-start.1 = (s32[64,64]{1,0:T(8,128)S(1)}, s32[64,64]{1,0:T(8,128)}, u32[]{:S(2)}) copy-start(s32[64,64]{1,0:T(8,128)} %param.15) | copy-start | bytes 49156
  24.3 332.5 %reduce-scatter.2.cloned.1.call-start = ((), (), s32[]{:S(2)}) async-start(), calls=%async_computation.2 | async-start | bytes 4718592 | tf_op jit(solution)/shard_map/reduce_scatter | solution.py:77
  138.7 3.1 copy-start.3
  144.6 1.0 copy-start.4
  146.4 3.1 copy-start.3
  154.1 3.1 copy-start.3
  160.1 1.0 copy-start.4
  161.8 3.1 copy-start.3
  167.8 1.0 copy-start.4
  169.5 3.1 copy-start.3
  175.5 1.0 copy-start.4
  177.2 3.1 copy-start.3
  183.2 1.0 copy-start.4
  184.9 3.1 copy-start.3
  192.7 3.1 copy-start.3
  198.6 1.0 copy-start.4
  200.4 3.1 copy-start.3
  206.4 1.0 copy-start.4
  208.1 3.1 copy-start.3
  214.1 1.0 copy-start.4
  215.8 3.1 copy-start.3
  223.5 3.1 copy-start.3
  231.2 3.1 copy-start.3
  237.2 1.0 copy-start.4
  238.9 3.1 copy-start.3
  244.9 1.0 copy-start.4
  246.6 3.1 copy-start.3
  252.6 1.0 copy-start.4
  254.4 3.1 copy-start.3
  (5 other events, 4.9 us)
Sparse Core Ops, SparseCore 0:
  24.5 113.4 all-gather.2
  268.3 88.4 reduce-scatter.1
where the time goes:
time: 365 us; the launch traced here: 364 us
  waiting for transfers between devices  175 us (48%)
  matrix products  112 us (31%)
  blocking collectives  26.2 us (7%)
  local copies, waits for them, and re-layouts  17.9 us (5%)
  other arithmetic  17.9 us (5%)
  between operations  13.5 us (4%)
    reduce_scatter x1, waiting for transfers between devices, per_device(): lax.psum_scatter(jnp.einsum('rhd,hdo->ro', attended_rows, out_weight, pre...  88.6 us
    all_gather x1, waiting for transfers between devices, per_device(): lax.all_gather(kv_local, 'ctx', axis=0, tiled=True)  86.8 us
    dot_general x16, matrix products, score_block(): jnp.einsum('hrk,khd->hrd', weights.astype(jnp.bfloat16), value_rows, pref...  45.8 us
    dot_general x16, matrix products, score_block(): jnp.einsum('rhd,khd->hrk', queries, key_rows, preferred_element_type=jnp....  32.2 us
    all_gather x1, blocking collectives, per_device(): lax.all_gather(clip_of, 'ctx', axis=0, tiled=True)  26.2 us
    reduce_sum x16, other arithmetic, score_block(): totals = totals * factor + jnp.sum(weights, axis=2)  16.6 us
    while x80, local copies, waits for them, and re-layouts  15.5 us
    dot_general x16, matrix products, score_block(): jnp.dot(query_vis, key_hot.T, precision=lax.Precision.HIGHEST) > 0.5  10.6 us
  transfers between devices with their start and end apart: 2, of which 2 were waited for; matrix products, arithmetic and copies ran while one was open for 0% of the time, Pallas kernels for 0%

commit v1 on v0

--- a/solution.py
+++ b/solution.py
@@ -69,7 +69,9 @@
     )
     kv_all, clips_all = (
         lax.all_gather(kv_local, "ctx", axis=0, tiled=True),
-        lax.all_gather(clip_of, "ctx", axis=0, tiled=True),
+        jnp.concatenate(
+            lax.all_to_all(jnp.stack([clip_of] * lax.axis_size("ctx")), "ctx", 0, 0), axis=0
+        ),
     )
     final = fold_keys(initial, kv_all, clips_all, queries, query_vis, score_scale)
     attended = (final[2] / final[1][:, :, None]).astype(jnp.bfloat16)

time: 365 us -> 348 us (0.953)
  blocking collectives: 26.2 us -> 0 us
  waiting for transfers between devices: 175 us -> 193 us
  local copies, waits for them, and re-layouts: 17.9 us -> 3.16 us
  starting transfers between devices: 0.04 us -> 8.48 us
    all_gather x1 -> x0, blocking collectives: 26.2 us -> none  [per_device(): lax.all_gather(clip_of, 'ctx', axis=0, tiled=True)]
    while x80 -> x16, local copies, waits for them, and re-layouts: 15.5 us -> 0.04 us
    all_gather x1, waiting for transfers between devices: 86.8 us -> 97.1 us  [per_device(): lax.all_gather(kv_local, 'ctx', axis=0, tiled=True)]
    all_to_all x0 -> x1, starting transfers between devices: none -> 8.44 us  [per_device(): lax.all_to_all(jnp.stack([clip_of] * lax.axis_size('ctx')), 'ctx', 0, 0)]
    all_to_all x0 -> x1, waiting for transfers between devices: none -> 6.8 us  [per_device(): lax.all_to_all(jnp.stack([clip_of] * lax.axis_size('ctx')), 'ctx', 0, 0)]
  transfers between devices with their start and end apart: 2 -> 3, of which waited for: 2 -> 3; matrix products, arithmetic and copies ran while one was open for 0% -> 0% of each run, Pallas kernels for 0% -> 0%
where the time goes in v1:
time: 348 us; the launch traced here: 346 us
  waiting for transfers between devices  193 us (55%)
  matrix products  110 us (32%)
  other arithmetic  17.9 us (5%)
  between operations  13.5 us (4%)
  starting transfers between devices  8.48 us (2%)
    all_gather x1, waiting for transfers between devices, per_device(): lax.all_gather(kv_local, 'ctx', axis=0, tiled=True)  97.1 us
    reduce_scatter x1, waiting for transfers between devices, per_device(): lax.psum_scatter(jnp.einsum('rhd,hdo->ro', attended_rows, out_weight, pre...  88.6 us
    dot_general x16, matrix products, score_block(): jnp.einsum('hrk,khd->hrd', weights.astype(jnp.bfloat16), value_rows, pref...  45.8 us
    dot_general x16, matrix products, score_block(): jnp.einsum('rhd,khd->hrk', queries, key_rows, preferred_element_type=jnp....  30.9 us
    reduce_sum x16, other arithmetic, score_block(): totals = totals * factor + jnp.sum(weights, axis=2)  16.6 us
    dot_general x16, matrix products, score_block(): jnp.dot(query_vis, key_hot.T, precision=lax.Precision.HIGHEST) > 0.5  10.6 us
    dot_general x1, matrix products, per_device(): jnp.einsum('td,dchk->tchk', moduled, qkv_weight, preferred_element_type=j...  10.1 us
    all_to_all x1, starting transfers between devices, per_device(): lax.all_to_all(jnp.stack([clip_of] * lax.axis_size('ctx')), 'ctx', 0, 0)  8.44 us
  transfers between devices with their start and end apart: 3, of which 3 were waited for; matrix products, arithmetic and copies ran while one was open for 0% of the time, Pallas kernels for 0%

profile of v1, /device:TPU:1, one launch (start us, length us, event | category | flops | bytes accessed | tf_op | source)
XLA Modules:
  0.0 346.2 jit_solution(17344369749537850653)
XLA Ops:
  7.5 5.6 %fusion.20 = bf16[512,4096,1,1]{1,0,3,2:T(8,128)(2,1)S(1)} fusion(f32[16,4096]{1,0:T(8,128)S(1)} %copy-done, bf16[512,4096]{1,0:T(8,128)(2,1)} %param.9, s32[512]{0:T(512)S(1)} %select_reduce_fusion), kind=kOutput, calls=%fused_computation.29 | convolution fusion | flops 411049984 | bytes 8652800 | tf_op jit(solution)/shard_map/dot_general | solution.py:54
  13.1 10.1 %fusion.21 = bf16[512,3,4,128]{3,0,2,1:T(8,128)(2,1)S(1)} fusion(bf16[512,4096,1,1]{1,0,3,2:T(8,128)(2,1)S(1)} %fusion.20, bf16[4096,3,4,128]{3,2,1,0:T(4,128)(2,1)} %param.10), kind=kOutput, calls=%fused_computation.30 | convolution fusion | flops 6443237376 | bytes 18350080 | tf_op jit(solution)/shard_map/td,dchk->tchk/dot_general | solution.py:56
  24.9 8.4 %all-to-all-start = ((s32[16,1,512]{2,1,0:T(1,128)}), s32[16,1,512]{2,1,0:T(1,128)S(1)}, u32[]{:S(2)}, u32[]{:S(2)}) async-start(s32[16,1,512]{2,1,0:T(1,128)} %stack.2), calls=%async_computation | async-start | bytes 65536 | tf_op jit(solution)/shard_map/all_to_all | solution.py:73
  33.9 6.8 %all-to-all-done = s32[16,1,512]{2,1,0:T(1,128)S(1)} async-done(((s32[16,1,512]{2,1,0:T(1,128)}), s32[16,1,512]{2,1,0:T(1,128)S(1)}, u32[]{:S(2)}, u32[]{:S(2)}) %all-to-all-start) | async-done | bytes 32800 | tf_op jit(solution)/shard_map/all_to_all | solution.py:73
  40.7 97.1 %all-gather.2.cloned.1.call-done = bf16[8192,2,4,128]{3,0,2,1:T(8,128)(2,1)} async-done(((bf16[512,2,4,128]{3,0,2,1:T(8,128)(2,1)}), bf16[8192,2,4,128]{3,0,2,1:T(8,128)(2,1)}) %all-gather.2.cloned.1.call-update) | async-done | bytes 16777232 | tf_op jit(solution)/shard_map/all_gather | solution.py:71
  137.8 106.7 %while.18 = (s32[]{:T(128)}, f32[4,512]{1,0:T(4,128)S(1)}, f32[4,512]{1,0:T(4,128)S(1)}, f32[4,512,128]{2,1,0:T(8,128)S(1)}, s32[8192]{0:T(1024)S(1)}, /*index=5...) while((s32[]{:T(128)}, f32[4,512]{1,0:T(4,128)S(1)}, ...), condition=%wide.region_4.5_spmd.clone, body=%wide.region_1.4_spmd.clone.sunk | while | flops 752920576 | bytes 17570012 | solution.py:41
  141.5 2.9 fusion.49
  145.2 1.9 fusion.46
  148.2 2.9 fusion.49
  151.9 1.9 fusion.46
  154.9 2.9 fusion.49
  158.5 1.9 fusion.46
  161.6 2.9 fusion.49
  165.2 1.9 fusion.46
  168.2 2.9 fusion.49
  171.9 1.9 fusion.46
  174.9 2.9 fusion.49
  178.5 1.9 fusion.46
  181.6 2.9 fusion.49
  185.2 1.9 fusion.46
  188.2 2.9 fusion.49
  191.9 1.9 fusion.46
  194.9 2.9 fusion.49
  201.6 2.9 fusion.49
  208.2 2.9 fusion.49
  214.9 2.9 fusion.49
  221.6 2.9 fusion.49
  228.3 2.9 fusion.49
  234.9 2.9 fusion.49
  241.6 2.9 fusion.49
  244.5 6.2 %bitcast_convert_fusion = bf16[512,4096]{1,0:T(8,128)(2,1)} fusion(bf16[4,128,4096]{2,1,0:T(8,128)(2,1)} %param.11, f32[4,512,128]{2,1,0:T(8,128)S(1)} %get-tuple-element.145, f32[4,512]{1,0:T(4,128)S(1)} %get-tuple-element.146), kind=kOutput, calls=%fused_computation.27 | convolution fusion | flops 2150105088 | bytes 9445376 | tf_op jit(solution)/shard_map/rhd,hdo->ro/dot_general | solution.py:80
  250.7 88.6 %reduce-scatter.2.cloned.1.call-done = bf16[64,4096]{1,0:T(8,128)(2,1)} async-done(((bf16[512,4096]{1,0:T(8,128)(2,1)}), bf16[64,4096]{1,0:T(8,128)(2,1)}) %reduce-scatter.2.cloned.1.call-update) | async-done | bytes 524304 | tf_op jit(solution)/shard_map/reduce_scatter | solution.py:79
  (122 shorter events, 47.6 us)
Async XLA Ops:
  6.5 1.0 copy-start
  6.5 131.2 %all-gather.2.cloned.1.call-start = ((), (), s32[]{:S(2)}) async-start(), calls=%async_computation.2 | async-start | bytes 17825792 | tf_op jit(solution)/shard_map/all_gather | solution.py:71
  13.1 11.2 %copy-start.2 = (s32[512]{0:T(512)S(1)}, s32[512]{0:T(512)}, u32[]{:S(2)}) copy-start(s32[512]{0:T(512)} %param.14) | copy-start | bytes 6148
  23.2 10.3 %copy-start.1 = (s32[64,64]{1,0:T(8,128)S(1)}, s32[64,64]{1,0:T(8,128)}, u32[]{:S(2)}) copy-start(s32[64,64]{1,0:T(8,128)} %param.15) | copy-start | bytes 49156
  24.9 15.8 %all-to-all-start = ((s32[16,1,512]{2,1,0:T(1,128)}), s32[16,1,512]{2,1,0:T(1,128)S(1)}, u32[]{:S(2)}, u32[]{:S(2)}) async-start(s32[16,1,512]{2,1,0:T(1,128)} %stack.2), calls=%async_computation | async-start | bytes 65536 | tf_op jit(solution)/shard_map/all_to_all | solution.py:73
  33.4 305.9 %reduce-scatter.2.cloned.1.call-start = ((), (), s32[]{:S(2)}) async-start(), calls=%async_computation.3 | async-start | bytes 4718592 | tf_op jit(solution)/shard_map/reduce_scatter | solution.py:79
Sparse Core Ops, SparseCore 0:
  24.4 113.3 all-gather.1
  250.8 88.4 reduce-scatter.1
